TPU v7x, 32 devices: a whole 2x2x4 slice. The times are simulated.
32 devices in a mesh: gx: 2 (over core), gy: 2 (over x), gz: 8 (over z, y).
Axes of the slice: x: 2, y: 2, z: 4, core: 2. Of those that a mesh axis runs over, the one named last changes fastest.
Arguments:
- charges: bfloat16 [32, 48, 2048], P('gx', 'gy', 'gz'), may hold values from -6 to 6
- kernel_fine: bfloat16 [9, 9, 9], replicated, may hold values from -0.21875 to 0.21875
- kernel_mid: bfloat16 [9, 9, 9], replicated, may hold values from -0.21875 to 0.21875
- gauss_width: float32 [8], replicated, may hold values from 1 to 64
- gauss_weight: float32 [8], replicated, may hold values from 0.25 to 2
Outputs:
- potential: float32 [32, 48, 2048], P('gx', 'gy', 'gz')
All inputs are finite; a program needn't handle non-finite values.
Results may differ from a plain program's by a relative error of at most 0.002.
Values may be sent and summed in bfloat16 or wider, within the bound.
No kernel may reach another device: no remote copies, remote signals or barrier semaphores. Data moves between devices by JAX's collectives and lax.ppermute only.
A program may use at most 384 MiB of HBM per device.

v0:
```python
import jax
import jax.numpy as jnp
from jax import lax
from jax.sharding import PartitionSpec as P

M = 16


def padded_2(cells, sides, width):
    for axis, dim in sides:
        count = lax.axis_size(axis)
        ends = count - 1
        head = lax.slice_in_dim(cells, 0, width, axis=dim)
        tail = lax.slice_in_dim(cells, cells.shape[dim] - width, cells.shape[dim], axis=dim)
        cells = jnp.concatenate(
            [
                lax.ppermute(tail, axis, [(i, (i + 1) % count) for i in range(ends)]),
                cells,
                lax.ppermute(head, axis, [((i + 1) % count, i) for i in range(ends)]),
            ],
            axis=dim,
        )
    return cells


def stencil(offset):
    value = jnp.zeros(offset.shape, jnp.float32)
    value = jnp.where(jnp.abs(offset) == 1, 9.0 / 16.0, value)
    value = jnp.where(offset == 0, 1.0, value)
    value = jnp.where(jnp.abs(offset) == 3, -1.0 / 16.0, value)
    return value


def restrict_band(rows, cols, margin):
    row_ids = jnp.arange(rows, dtype=jnp.int32)[:, None]
    col_ids = jnp.arange(cols, dtype=jnp.int32)[None, :]
    return stencil(col_ids - margin - 2 * row_ids)


def prolong_band(rows, cols):
    row_ids = jnp.arange(rows, dtype=jnp.int32)[:, None]
    col_ids = jnp.arange(cols, dtype=jnp.int32)[None, :]
    return stencil(row_ids - 2 * col_ids + 4)


def restrict_padded(padded, sizes, margin):
    highest = lax.Precision.HIGHEST
    band_x = restrict_band(sizes[0], padded.shape[0], margin).astype(jnp.bfloat16)
    band_y = restrict_band(sizes[1], padded.shape[1], margin)
    band_z = restrict_band(sizes[2], padded.shape[2], margin)
    field = jnp.einsum("ia,abcm->ibcm", band_x, padded, preferred_element_type=jnp.float32)
    field = jnp.einsum("jb,ibcm->ijcm", band_y, field, precision=highest)
    field = jnp.einsum("kc,ijcm->ijkm", band_z, field, precision=highest)
    return field


def prolong_ext(field, sizes):
    highest = lax.Precision.HIGHEST
    field = jnp.einsum(
        "ia,abcm->ibcm", prolong_band(sizes[0], field.shape[0]), field, precision=highest
    )
    field = jnp.einsum(
        "jb,ibcm->ijcm", prolong_band(sizes[1], field.shape[1]), field, precision=highest
    )
    field = jnp.einsum(
        "kc,ijcm->ijkm", prolong_band(sizes[2], field.shape[2]), field, precision=highest
    )
    return field


def correlate(padded, kernel, out_sizes):
    reach = jnp.arange(9, dtype=jnp.int32)[:, None, None]
    lag_y = (
        jnp.arange(padded.shape[1], dtype=jnp.int32)[:, None]
        - jnp.arange(out_sizes[1], dtype=jnp.int32)[None, :]
    )
    lag_z = (
        jnp.arange(padded.shape[2], dtype=jnp.int32)[:, None]
        - jnp.arange(out_sizes[2], dtype=jnp.int32)[None, :]
    )
    pick_y = (lag_y[None] == reach).astype(jnp.bfloat16)
    pick_z = (lag_z[None] == reach).astype(jnp.bfloat16)
    total = jnp.zeros((out_sizes[0], out_sizes[1], out_sizes[2], padded.shape[3]), jnp.float32)
    for offset in range(9):
        table = jnp.einsum(
            "bc,bpy,cqz->pqyz", kernel[offset], pick_y, pick_z, preferred_element_type=jnp.float32
        ).astype(jnp.bfloat16)
        total = total + jnp.einsum(
            "xpqm,pqyz->xyzm",
            padded[offset : offset + out_sizes[0]],
            table,
            preferred_element_type=jnp.float32,
        )
    return total


def gaussian_table(first_row, rows, cols, whole, gauss_width):
    row_pos = first_row + jnp.arange(rows, dtype=jnp.int32)
    col_pos = jnp.arange(cols, dtype=jnp.int32)
    spread = (row_pos[:, None] - col_pos[None, :]).astype(jnp.float32)
    width = gauss_width[:, None, None]
    table = jnp.exp(-jnp.square(spread[None] / width)) / jnp.sqrt(width)
    inside = (row_pos >= 0) & (row_pos < whole)
    return jnp.where(inside[None, :, None], table, 0.0)


def inside_mask(position, count, local, rim):
    spots = position * local - rim + jnp.arange(local + 2 * rim, dtype=jnp.int32)
    return ((spots >= 0) & (spots < local * count)).astype(jnp.float32)


def per_device(charges, kernel_fine, kernel_mid, gauss_width, gauss_weight):
    highest = lax.Precision.HIGHEST
    size_x, size_y, flat = charges.shape
    members = M
    size_z = flat // members
    field = charges.reshape(size_x, size_y, size_z, members)
    padded = padded_2(field, (("gx", 0), ("gy", 1), ("gz", 2)), 4)
    short_fine = correlate(padded, kernel_fine, (size_x, size_y, size_z))
    mid_sizes = (size_x // 2, size_y // 2, size_z // 2)
    q_mid = restrict_padded(padded, mid_sizes, 4).astype(jnp.bfloat16)
    mid_padded = padded_2(q_mid, (("gx", 0), ("gy", 1), ("gz", 2)), 6)
    short_mid = correlate(
        mid_padded, kernel_mid, (mid_sizes[0] + 4, mid_sizes[1] + 4, mid_sizes[2] + 4)
    )
    top_x, top_y, top_z = (size_x // 4, size_y // 4, size_z // 4)
    q_top = restrict_padded(mid_padded, (top_x, top_y, top_z), 6)
    count_x = lax.axis_size("gx")
    count_y = lax.axis_size("gy")
    count_z = lax.axis_size("gz")
    index_x = lax.axis_index("gx")
    index_y = lax.axis_index("gy")
    index_z = lax.axis_index("gz")
    whole_x = top_x * count_x
    whole_y = top_y * count_y
    whole_z = top_z * count_z
    first_x = index_x * top_x - 3
    first_y = index_y * top_y - 3
    first_z = index_z * top_z - 3
    scaled = gauss_weight[:, None, None]
    piece = lax.all_gather(q_top, "gx", axis=0, tiled=True)
    table = gaussian_table(first_x, top_x + 6, piece.shape[0], whole_x, gauss_width) * scaled
    section = jnp.einsum("gia,abcm->gibcm", table, piece, precision=highest)
    piece = lax.all_gather(section, "gy", axis=2, tiled=True)
    table = gaussian_table(first_y, top_y + 6, piece.shape[2], whole_y, gauss_width)
    section = jnp.einsum("gjb,gibcm->gijcm", table, piece, precision=highest)
    piece = lax.all_gather(section, "gz", axis=3, tiled=True)
    table = gaussian_table(first_z, top_z + 6, piece.shape[3], whole_z, gauss_width)
    section = jnp.einsum("gkc,gijcm->gijkm", table, piece, precision=highest)
    phi_top = jnp.sum(section, axis=0)
    ext_sizes = (mid_sizes[0] + 4, mid_sizes[1] + 4, mid_sizes[2] + 4)
    phi_mid = short_mid + prolong_ext(phi_top, ext_sizes)
    mask_x = inside_mask(index_x, count_x, mid_sizes[0], 2)
    mask_y = inside_mask(index_y, count_y, mid_sizes[1], 2)
    mask_z = inside_mask(index_z, count_z, mid_sizes[2], 2)
    phi_mid = (
        phi_mid
        * mask_x[:, None, None, None]
        * mask_y[None, :, None, None]
        * mask_z[None, None, :, None]
    )
    potential = short_fine + prolong_ext(phi_mid, (size_x, size_y, size_z))
    return potential.reshape(size_x, size_y, size_z * members)


def solution(mesh):
    placed = (P("gx", "gy", "gz"), P(), P(), P(), P())
    return jax.shard_map(
        per_device, mesh=mesh, in_specs=placed, out_specs=P("gx", "gy", "gz"), check_vma=False
    )
```

profile of v0, /device:TPU:0, one launch (start us, length us, event | category | flops | bytes accessed | tf_op | source)
XLA Modules:
  0.0 811.1 jit_solution(4082454548919218295)
XLA Ops:
  55.6 4.9 collective-permute-start.2
  110.3 16.5 %collective-permute-done.4 = bf16[24,32,4,16]{1,3,2,0:T(8,128)(2,1)S(1)} collective-permute-done((bf16[24,32,4,16]{1,3,2,0:T(8,128)(2,1)S(1)}, bf16[24,32,4,16]{1,3,2,0:T(8,128)(2,1)S(1)}, u32[]{:S(2)}, u32[]{:S(2)}) %collective-permute-start.4) | collective-permute-done | bytes 98336 | tf_op jit(solution)/shard_map/ppermute | solution.py:17
  130.9 7.8 fusion.60
  138.7 7.4 fusion.212
  150.2 6.8 fusion.10
  157.1 4.9 fusion.12
  162.0 4.9 fusion.14
  166.9 4.8 fusion.16
  171.7 4.8 fusion.18
  176.5 5.1 fusion.6
  187.8 4.8 fusion.8
  200.6 5.2 collective-permute-start.10
  209.5 6.0 fusion.4
  215.5 10.6 %collective-permute-done.10 = bf16[20,24,6,16]{1,3,2,0:T(8,128)(2,1)} collective-permute-done((bf16[20,24,6,16]{1,3,2,0:T(8,128)(2,1)S(1)}, bf16[20,24,6,16]{1,3,2,0:T(8,128)(2,1)}, u32[]{:S(2)}, u32[]{:S(2)}) %collective-permute-start.10) | collective-permute-done | bytes 92192 | tf_op jit(solution)/shard_map/ppermute | solution.py:17
  231.2 5.7 pad_maximum_fusion
  236.9 6.0 copy.65
  245.0 4.7 convolution_bitcast_fusion.2
  253.4 37.3 %all_gather.10 = f32[8,10,12,4,16]{4,1,3,2,0:T(8,128)S(1)} all-gather(f32[8,10,6,4,16]{4,1,3,2,0:T(8,128)S(1)} %fusion.98), channel_id=1, replica_groups=mesh['gx'=2,'gy'=2,'gz'=8] {'gy'}, dimensions={2}, use_global_device_ids=true | all-gather | bytes 368640 | tf_op jit(solution)/shard_map/all_gather | solution.py:144
  290.8 6.8 fusion.33
  314.3 385.5 %all-gather.2.cloned.1.call-done = f32[8,10,12,32,16]{2,4,3,1,0:T(8,128)} async-done(((f32[8,10,12,4,16]{2,4,3,1,0:T(8,128)}), f32[8,10,12,32,16]{2,4,3,1,0:T(8,128)}) %all-gather.2.cloned.1.call-update) | async-done | bytes 1966096 | tf_op jit(solution)/shard_map/all_gather | solution.py:147
  699.9 26.4 %copy.70 = f32[8,10,12,32,16]{4,3,0,2,1:T(8,128)} copy(f32[8,10,12,32,16]{2,4,3,1,0:T(8,128)} %all-gather.2.cloned.1.call-done) | data formatting | bytes 3932160 | tf_op jit(solution)/shard_map/all_gather | solution.py:147
  726.3 28.3 %convolution_bitcast_fusion = f32[10,12,10,16]{2,3,1,0:T(8,128)} fusion(f32[8,10,12,32,16]{4,3,0,2,1:T(8,128)} %copy.70, f32[8]{0:T(128)S(1)} %sqrt.6, f32[8]{0:T(128)S(1)} %copy-done.26, f32[10,32]{1,0:T(8,128)S(1)} %subtract_convert_fusion, pred[10]{0:T(512)(128)(4,1)S(1)} %compare_and_fusion), kind=kOutput, calls=%fused_computation.105 | convolution fusion | flops 58995200 | bytes 2044234 | tf_op jit(solution)/shard_map/gkc,gijcm->gijkm/dot_general | solution.py:149
  774.5 5.7 fusion.75
  789.5 9.7 %bitcast_add_fusion = f32[16,24,16,16]{1,3,0,2:T(8,128)} fusion(f32[24,16,16,16,1]{0,3,4,2,1:T(8,128)} %fusion.4, f32[24,16,16,16,1]{0,3,4,2,1:T(8,128)} %fusion.6, f32[24,16,16,16,1]{0,3,4,2,1:T(8,128)} %fusion.8, f32[24,16,16,16,1]{0,3,4,2,1:T(8,128)S(1)} %copy-done.28, f32[24,16,16,16,1]{0,3,4,2,1:T(8,128)} %fusion.12, ...), kind=kOutput, calls=%fused_computation.33 | convolution fusion | flops 151879680 | bytes 11272192 | tf_op jit(solution)/shard_map/xpqm,pqyz->xyzm/dot_general | solution.py:88
  (181 shorter events, 185.9 us)
Async XLA Ops:
  6.5 7.5 copy-start.24
  6.5 693.3 %all-gather.2.cloned.1.call-start = ((), (), s32[]{:S(2)}) async-start(), calls=%async_computation | async-start | bytes 23592960 | tf_op jit(solution)/shard_map/all_gather | solution.py:147
  7.6 42.0 %collective-permute-start = (bf16[4,24,16,16]{1,3,2,0:T(8,128)(2,1)S(1)}, bf16[4,24,16,16]{1,3,2,0:T(8,128)(2,1)S(1)}, u32[]{:S(2)}, u32[]{:S(2)}) collective-permute-start(bf16[4,24,16,16]{1,3,2,0:T(8,128)(2,1)S(1)} %bitcast.636), channel_id=1, source_target_pairs={{0,16},{1,17},{2,18},{3,19},{4,20},{5,21},{6,22},{7,23},{8,24},{9,... | collective-permute-start | bytes 147464 | tf_op jit(solution)/shard_map/ppermute | solution.py:17
  10.2 39.4 %collective-permute-start.1 = (bf16[4,24,16,16]{1,3,2,0:T(8,128)(2,1)S(1)}, bf16[4,24,16,16]{1,3,2,0:T(8,128)(2,1)S(1)}, u32[]{:S(2)}, u32[]{:S(2)}) collective-permute-start(bf16[4,24,16,16]{1,3,2,0:T(8,128)(2,1)S(1)} %bitcast.637), channel_id=1, source_target_pairs={{16,0},{17,1},{18,2},{19,3},{20,4},{21,5},{22,6},{23,7},{24,8},{25... | collective-permute-start | bytes 147464 | tf_op jit(solution)/shard_map/ppermute | solution.py:19
  51.9 12.8 %copy-start.26 = (f32[8]{0:T(128)S(1)}, f32[8]{0:T(128)}, u32[]{:S(2)}) copy-start(f32[8]{0:T(128)} %param.8) | copy-start | bytes 100
  55.6 39.5 %collective-permute-start.2 = (bf16[24,4,16,16]{0,3,2,1:T(8,128)(2,1)S(1)}, bf16[24,4,16,16]{0,3,2,1:T(8,128)(2,1)}, u32[]{:S(2)}, u32[]{:S(2)}) collective-permute-start(bf16[24,4,16,16]{0,3,2,1:T(8,128)(2,1)S(1)} %copy.19), channel_id=1, source_target_pairs={{0,8},{1,9},{2,10},{3,11},{4,12},{5,13},{6,14},{7,15},{16,24},{17,... | collective-permute-start | bytes 147464 | tf_op jit(solution)/shard_map/ppermute | solution.py:17
  63.4 35.6 %collective-permute-start.3 = (bf16[24,4,16,16]{0,3,2,1:T(8,128)(2,1)}, bf16[24,4,16,16]{0,3,2,1:T(8,128)(2,1)}, u32[]{:S(2)}, u32[]{:S(2)}) collective-permute-start(bf16[24,4,16,16]{0,3,2,1:T(8,128)(2,1)} %copy.20), channel_id=1, source_target_pairs={{8,0},{9,1},{10,2},{11,3},{12,4},{13,5},{14,6},{15,7},{24,16},{25,... | collective-permute-start | bytes 147464 | tf_op jit(solution)/shard_map/ppermute | solution.py:19
  64.7 7.5 copy-start.6
  74.8 7.5 copy-start.5
  85.0 7.4 copy-start.4
  103.6 23.2 %copy-start = (bf16[24,4,16,16]{1,3,2,0:T(8,128)(2,1)S(1)}, bf16[24,4,16,16]{1,3,2,0:T(8,128)(2,1)}, u32[]{:S(2)}) copy-start(bf16[24,4,16,16]{1,3,2,0:T(8,128)(2,1)} %copy.22) | copy-start | bytes 147460
  105.5 21.2 %collective-permute-start.4 = (bf16[24,32,4,16]{1,3,2,0:T(8,128)(2,1)S(1)}, bf16[24,32,4,16]{1,3,2,0:T(8,128)(2,1)S(1)}, u32[]{:S(2)}, u32[]{:S(2)}) collective-permute-start(bf16[24,32,4,16]{1,3,2,0:T(8,128)(2,1)S(1)} %get-tuple-element.5), channel_id=1, source_target_pairs={{0,1},{1,2},{2,3},{3,4},{4,5},{5,6},{6,7},{8,9},{9,10},{10,11},{11... | collective-permute-start | bytes 294920 | tf_op jit(solution)/shard_map/ppermute | solution.py:17
  109.0 17.8 %collective-permute-start.5 = (bf16[24,32,4,16]{1,3,2,0:T(8,128)(2,1)S(1)}, bf16[24,32,4,16]{1,3,2,0:T(8,128)(2,1)S(1)}, u32[]{:S(2)}, u32[]{:S(2)}) collective-permute-start(bf16[24,32,4,16]{1,3,2,0:T(8,128)(2,1)S(1)} %get-tuple-element.6), channel_id=1, source_target_pairs={{1,0},{2,1},{3,2},{4,3},{5,4},{6,5},{7,6},{9,8},{10,9},{11,10},{12... | collective-permute-start | bytes 294920 | tf_op jit(solution)/shard_map/ppermute | solution.py:19
  129.1 9.6 %copy-start.1 = (bf16[24,32,24,16]{1,3,2,0:T(8,128)(2,1)}, bf16[24,32,24,16]{1,3,2,0:T(8,128)(2,1)S(1)}, u32[]{:S(2)}) copy-start(bf16[24,32,24,16]{1,3,2,0:T(8,128)(2,1)S(1)} %pad_maximum_fusion.1) | copy-start | bytes 1769476
  146.7 34.9 %collective-permute-start.6 = (bf16[6,12,8,16]{3,2,1,0:T(8,128)(2,1)S(1)}, bf16[6,12,8,16]{3,2,1,0:T(8,128)(2,1)S(1)}, u32[]{:S(2)}, u32[]{:S(2)}) collective-permute-start(bf16[6,12,8,16]{3,2,1,0:T(8,128)(2,1)S(1)} %get-tuple-element.13), channel_id=1, source_target_pairs={{0,16},{1,17},{2,18},{3,19},{4,20},{5,21},{6,22},{7,23},{8,24},{9,... | collective-permute-start | bytes 55304 | tf_op jit(solution)/shard_map/ppermute | solution.py:17
  148.6 8.4 %copy-start.2 = (bf16[24,32,24,16]{1,3,2,0:T(8,128)(2,1)S(1)}, bf16[24,32,24,16]{1,3,2,0:T(8,128)(2,1)}, u32[]{:S(2)}) copy-start(bf16[24,32,24,16]{1,3,2,0:T(8,128)(2,1)} %copy-done.1) | copy-start | bytes 1769476
  148.6 8.4 %copy-start.13 = (bf16[32,24,24,16,1]{0,3,2,1,4:T(8,128)(2,1)S(1)}, bf16[32,24,24,16,1]{0,3,2,1,4:T(8,128)(2,1)}, u32[]{:S(2)}) copy-start(bf16[32,24,24,16,1]{0,3,2,1,4:T(8,128)(2,1)} %convert_bitcast_fusion.5) | copy-start | bytes 1769476
  148.7 33.0 %collective-permute-start.7 = (bf16[6,12,8,16]{3,2,1,0:T(8,128)(2,1)S(1)}, bf16[6,12,8,16]{3,2,1,0:T(8,128)(2,1)S(1)}, u32[]{:S(2)}, u32[]{:S(2)}) collective-permute-start(bf16[6,12,8,16]{3,2,1,0:T(8,128)(2,1)S(1)} %get-tuple-element.14), channel_id=1, source_target_pairs={{16,0},{17,1},{18,2},{19,3},{20,4},{21,5},{22,6},{23,7},{24,8},{25... | collective-permute-start | bytes 55304 | tf_op jit(solution)/shard_map/ppermute | solution.py:19
  176.5 11.2 %copy-start.8 = (bf16[32,24,24,16,1]{0,3,2,1,4:T(8,128)(2,1)S(1)}, bf16[32,24,24,16,1]{0,3,2,1,4:T(8,128)(2,1)}, u32[]{:S(2)}) copy-start(bf16[32,24,24,16,1]{0,3,2,1,4:T(8,128)(2,1)} %convert_bitcast_fusion.3) | copy-start | bytes 1769476
  181.8 10.8 %collective-permute-start.8 = (bf16[20,6,8,16]{3,2,1,0:T(8,128)(2,1)S(1)}, bf16[20,6,8,16]{3,2,1,0:T(8,128)(2,1)S(1)}, u32[]{:S(2)}, u32[]{:S(2)}) collective-permute-start(bf16[20,6,8,16]{3,2,1,0:T(8,128)(2,1)S(1)} %get-tuple-element.11), channel_id=1, source_target_pairs={{0,8},{1,9},{2,10},{3,11},{4,12},{5,13},{6,14},{7,15},{16,24},{17,... | collective-permute-start | bytes 92168 | tf_op jit(solution)/shard_map/ppermute | solution.py:17
  186.5 10.6 %collective-permute-start.9 = (bf16[20,6,8,16]{3,2,1,0:T(8,128)(2,1)S(1)}, bf16[20,6,8,16]{3,2,1,0:T(8,128)(2,1)S(1)}, u32[]{:S(2)}, u32[]{:S(2)}) collective-permute-start(bf16[20,6,8,16]{3,2,1,0:T(8,128)(2,1)S(1)} %get-tuple-element.12), channel_id=1, source_target_pairs={{8,0},{9,1},{10,2},{11,3},{12,4},{13,5},{14,6},{15,7},{24,16},{25,... | collective-permute-start | bytes 92168 | tf_op jit(solution)/shard_map/ppermute | solution.py:19
  200.6 25.5 %collective-permute-start.10 = (bf16[20,24,6,16]{1,3,2,0:T(8,128)(2,1)S(1)}, bf16[20,24,6,16]{1,3,2,0:T(8,128)(2,1)}, u32[]{:S(2)}, u32[]{:S(2)}) collective-permute-start(bf16[20,24,6,16]{1,3,2,0:T(8,128)(2,1)S(1)} %copy.43), channel_id=1, source_target_pairs={{0,1},{1,2},{2,3},{3,4},{4,5},{5,6},{6,7},{8,9},{9,10},{10,11},{11... | collective-permute-start | bytes 276488 | tf_op jit(solution)/shard_map/ppermute | solution.py:17
  208.2 20.5 %collective-permute-start.11 = (bf16[20,24,6,16]{1,3,2,0:T(8,128)(2,1)}, bf16[20,24,6,16]{1,3,2,0:T(8,128)(2,1)}, u32[]{:S(2)}, u32[]{:S(2)}) collective-permute-start(bf16[20,24,6,16]{1,3,2,0:T(8,128)(2,1)} %copy.44), channel_id=1, source_target_pairs={{1,0},{2,1},{3,2},{4,3},{5,4},{6,5},{7,6},{9,8},{10,9},{11,10},{12... | collective-permute-start | bytes 276488 | tf_op jit(solution)/shard_map/ppermute | solution.py:19
  242.9 9.0 %copy-start.27 = (f32[8]{0:T(128)S(1)}, f32[8]{0:T(128)}, u32[]{:S(2)}) copy-start(f32[8]{0:T(128)} %param.9) | copy-start | bytes 100
  (18 other events, 62.2 us)
Sparse Core Ops, SparseCore 0:
  297.7 402.1 all-gather.1
where the time goes:
time: 821 us; the launch traced here: 811 us
  waiting for transfers between devices  417 us (51%)
  matrix products  188 us (23%)
  local copies, waits for them, and re-layouts  111 us (14%)
  blocking collectives  39.2 us (5%)
  starting transfers between devices  30.6 us (4%)
  between operations  14.3 us (2%)
  other arithmetic  11 us (1%)
    all_gather x1, waiting for transfers between devices, per_device(): piece = lax.all_gather(section, 'gz', axis=3, tiled=True)  386 us
    dot_general x18, matrix products, correlate(): jnp.einsum('xpqm,pqyz->xyzm', padded[offset:offset + out_sizes[0]], table...  74.3 us
    all_gather x1, blocking collectives, per_device(): piece = lax.all_gather(section, 'gy', axis=2, tiled=True)  37.3 us
    dot_general x18, matrix products, correlate(): jnp.einsum('bc,bpy,cqz->pqyz', kernel[offset], pick_y, pick_z, preferred_...  37 us
    convert_element_type x9, local copies, waits for them, and re-layouts, correlate(): table = jnp.einsum('bc,bpy,cqz->pqyz', kernel[offset], pick_y, pick_z, pr...  30.3 us
    dot_general x1, matrix products, per_device(): section = jnp.einsum('gkc,gijcm->gijkm', table, piece, precision=highest)  28.3 us
    ppermute x6, waiting for transfers between devices, padded_2(): lax.ppermute(tail, axis, [(i, (i + 1) % count) for i in range(ends)])  27.1 us
    all_gather x1, local copies, waits for them, and re-layouts, per_device(): piece = lax.all_gather(section, 'gz', axis=3, tiled=True)  26.4 us
  transfers between devices with their start and end apart: 13, of which 4 were waited for; matrix products, arithmetic and copies ran while one was open for 17% of the time, Pallas kernels for 0%

commit v1 on v0

--- a/solution.py
+++ b/solution.py
@@ -144,7 +144,15 @@
     piece = lax.all_gather(section, "gy", axis=2, tiled=True)
     table = gaussian_table(first_y, top_y + 6, piece.shape[2], whole_y, gauss_width)
     section = jnp.einsum("gjb,gibcm->gijcm", table, piece, precision=highest)
-    piece = lax.all_gather(section, "gz", axis=3, tiled=True)
+    ways, here = (lax.axis_size("gz"), lax.axis_index("gz"))
+    grown, reach_2 = (section, 1)
+    while reach_2 < ways:
+        theirs = lax.ppermute(grown, "gz", [(d, d ^ reach_2) for d in range(ways)])
+        mine_first = jnp.concatenate([grown, theirs], axis=3)
+        theirs_first = jnp.concatenate([theirs, grown], axis=3)
+        grown = jnp.where(here & reach_2 == 0, mine_first, theirs_first)
+        reach_2 = 2 * reach_2
+    piece = grown
     table = gaussian_table(first_z, top_z + 6, piece.shape[3], whole_z, gauss_width)
     section = jnp.einsum("gkc,gijcm->gijkm", table, piece, precision=highest)
     phi_top = jnp.sum(section, axis=0)

time: 821 us -> 887 us (1.080)
  waiting for transfers between devices: 417 us -> 461 us
  local copies, waits for them, and re-layouts: 111 us -> 143 us
  other arithmetic: 11 us -> 32.2 us
  between operations: 14.3 us -> 1.08 us
  matrix products: 188 us -> 175 us
  blocking collectives: 39.2 us -> 26.4 us
    ppermute x0 -> x3, waiting for transfers between devices: none -> 430 us  [per_device(): theirs = lax.ppermute(grown, 'gz', [(d, d ^ reach_2) for d in range(ways)])]
    all_gather x1 -> x0, waiting for transfers between devices: 386 us -> none  [per_device(): piece = lax.all_gather(section, 'gz', axis=3, tiled=True)]
    select_n x0 -> x3, local copies, waits for them, and re-layouts: none -> 33.6 us  [per_device(): grown = jnp.where(here & reach_2 == 0, mine_first, theirs_first)]
    all_gather x1 -> x0, local copies, waits for them, and re-layouts: 26.4 us -> none  [per_device(): piece = lax.all_gather(section, 'gz', axis=3, tiled=True)]
    ppermute x0 -> x3, local copies, waits for them, and re-layouts: none -> 20.4 us  [per_device(): theirs = lax.ppermute(grown, 'gz', [(d, d ^ reach_2) for d in range(ways)])]
    select_n x0 -> x2, other arithmetic: none -> 19.3 us  [per_device(): grown = jnp.where(here & reach_2 == 0, mine_first, theirs_first)]
    dot_general x1, matrix products: 28.3 us -> 15.3 us  [per_device(): section = jnp.einsum('gkc,gijcm->gijkm', table, piece, precision=highest)]
    all_gather x1, blocking collectives: 37.3 us -> 24.5 us  [per_device(): piece = lax.all_gather(section, 'gy', axis=2, tiled=True)]
  transfers between devices with their start and end apart: 13 -> 15, of which waited for: 4 -> 6; matrix products, arithmetic and copies ran while one was open for 17% -> 18% of each run, Pallas kernels for 0% -> 0%
where the time goes in v1:
time: 887 us; the launch traced here: 876 us
  waiting for transfers between devices  461 us (52%)
  matrix products  175 us (20%)
  local copies, waits for them, and re-layouts  143 us (16%)
  starting transfers between devices  37.2 us (4%)
  other arithmetic  32.2 us (4%)
  blocking collectives  26.4 us (3%)
    ppermute x3, waiting for transfers between devices, per_device(): theirs = lax.ppermute(grown, 'gz', [(d, d ^ reach_2) for d in range(ways)])  430 us
    dot_general x18, matrix products, correlate(): jnp.einsum('xpqm,pqyz->xyzm', padded[offset:offset + out_sizes[0]], table...  77.1 us
    dot_general x18, matrix products, correlate(): jnp.einsum('bc,bpy,cqz->pqyz', kernel[offset], pick_y, pick_z, preferred_...  37 us
    select_n x3, local copies, waits for them, and re-layouts, per_device(): grown = jnp.where(here & reach_2 == 0, mine_first, theirs_first)  33.6 us
    convert_element_type x9, local copies, waits for them, and re-layouts, correlate(): table = jnp.einsum('bc,bpy,cqz->pqyz', kernel[offset], pick_y, pick_z, pr...  30.4 us
    ppermute x6, waiting for transfers between devices, padded_2(): lax.ppermute(tail, axis, [(i, (i + 1) % count) for i in range(ends)])  26.6 us
    all_gather x1, blocking collectives, per_device(): piece = lax.all_gather(section, 'gy', axis=2, tiled=True)  24.5 us
    ppermute x6, starting transfers between devices, padded_2(): lax.ppermute(tail, axis, [(i, (i + 1) % count) for i in range(ends)])  22.6 us
  transfers between devices with their start and end apart: 15, of which 6 were waited for; matrix products, arithmetic and copies ran while one was open for 18% of the time, Pallas kernels for 0%

profile of v1, /device:TPU:0, one launch (start us, length us, event | category | flops | bytes accessed | tf_op | source)
XLA Modules:
  0.0 876.1 jit_solution(8756032401045333630)
XLA Ops:
  105.5 15.9 %collective-permute-done.4 = bf16[24,32,4,16]{1,3,2,0:T(8,128)(2,1)S(1)} collective-permute-done((bf16[24,32,4,16]{1,3,2,0:T(8,128)(2,1)S(1)}, bf16[24,32,4,16]{1,3,2,0:T(8,128)(2,1)S(1)}, u32[]{:S(2)}, u32[]{:S(2)}) %collective-permute-start.4) | collective-permute-done | bytes 98336 | tf_op jit(solution)/shard_map/ppermute | solution.py:17
  125.7 7.8 fusion.62
  133.5 7.4 fusion.209
  145.0 6.6 fusion.10
  171.0 5.2 fusion.20
  204.1 6.0 fusion.6
  210.1 10.8 %collective-permute-done.10 = bf16[20,24,6,16]{1,3,2,0:T(8,128)(2,1)} collective-permute-done((bf16[20,24,6,16]{1,3,2,0:T(8,128)(2,1)S(1)}, bf16[20,24,6,16]{1,3,2,0:T(8,128)(2,1)}, u32[]{:S(2)}, u32[]{:S(2)}) %collective-permute-start.10) | collective-permute-done | bytes 92192 | tf_op jit(solution)/shard_map/ppermute | solution.py:17
  225.8 5.7 pad_maximum_fusion
  231.6 6.0 copy.65
  247.4 24.5 %all_gather.7 = f32[8,10,12,4,16]{4,0,3,1,2:T(8,128)S(1)} all-gather(f32[8,10,6,4,16]{4,0,3,1,2:T(8,128)S(1)} %fusion.103), channel_id=1, replica_groups=mesh['gx'=2,'gy'=2,'gz'=8] {'gy'}, dimensions={2}, use_global_device_ids=true | all-gather | bytes 368640 | tf_op jit(solution)/shard_map/all_gather | solution.py:144
  271.9 5.2 fusion.35
  294.9 31.2 %collective-permute-done.12 = f32[8,10,12,4,16]{4,0,3,2,1:T(8,128)} collective-permute-done((f32[8,10,12,4,16]{4,0,3,2,1:T(8,128)}, f32[8,10,12,4,16]{4,0,3,2,1:T(8,128)}, u32[]{:S(2)}, u32[]{:S(2)}) %collective-permute-start.12) | collective-permute-done | bytes 245792 | tf_op jit(solution)/shard_map/ppermute | solution.py:150
  330.3 5.3 maximum_select_fusion.2
  335.7 7.4 copy.74
  347.8 81.1 %collective-permute-done.13 = f32[8,10,12,8,16]{4,3,2,1,0:T(8,128)} collective-permute-done((f32[8,10,12,8,16]{4,3,2,1,0:T(8,128)}, f32[8,10,12,8,16]{4,3,2,1,0:T(8,128)}, u32[]{:S(2)}, u32[]{:S(2)}) %collective-permute-start.13) | collective-permute-done | bytes 491552 | tf_op jit(solution)/shard_map/ppermute | solution.py:150
  428.9 7.0 copy.75
  436.0 13.9 %maximum_select_fusion = f32[8,10,12,16,16]{2,4,3,1,0:T(8,128)} fusion(f32[8,10,12,8,16]{2,4,3,1,0:T(8,128)} %copy.75, f32[8,10,12,8,16]{2,4,3,1,0:T(8,128)} %maximum_select_fusion.2, pred[]{:T(512)S(6)} %eq.413), kind=kLoop, calls=%fused_computation | loop fusion | flops 737280 | bytes 1966081 | tf_op jit(solution)/shard_map/jit(_where)/select_n | solution.py:153
  449.9 13.1 %copy.77 = f32[8,10,12,16,16]{4,3,2,1,0:T(8,128)} copy(f32[8,10,12,16,16]{2,4,3,1,0:T(8,128)} %maximum_select_fusion) | data formatting | bytes 1966080 | tf_op jit(solution)/shard_map/jit(_where)/select_n | solution.py:153
  470.5 13.1 %copy.78 = f32[8,10,12,16,16]{3,4,2,1,0:T(8,128)} copy(f32[8,10,12,16,16]{2,4,3,1,0:T(8,128)} %maximum_select_fusion) | data formatting | bytes 1966080 | tf_op jit(solution)/shard_map/jit(_where)/select_n | solution.py:153
  483.6 318.1 %collective-permute-done.14 = f32[8,10,12,16,16]{4,3,2,1,0:T(8,128)} collective-permute-done((f32[8,10,12,16,16]{4,3,2,1,0:T(8,128)}, f32[8,10,12,16,16]{4,3,2,1,0:T(8,128)}, u32[]{:S(2)}, u32[]{:S(2)}) %collective-permute-start.14) | collective-permute-done | bytes 983072 | tf_op jit(solution)/shard_map/ppermute | solution.py:150
  801.7 9.1 %copy.79 = f32[8,10,12,16,16]{3,4,2,1,0:T(8,128)} copy(f32[8,10,12,16,16]{4,3,2,1,0:T(8,128)} %collective-permute-done.14) | data formatting | bytes 1966080 | tf_op jit(solution)/shard_map/ppermute | solution.py:150
  810.8 15.3 %fusion.65 = f32[10,12,10,16]{2,3,0,1:T(8,128)} fusion(f32[8]{0:T(128)S(1)} %sqrt.6, f32[8]{0:T(128)S(1)} %copy-done.27, f32[10,32]{1,0:T(8,128)S(1)} %subtract_convert_fusion, pred[10]{0:T(512)(128)(4,1)S(1)} %copy-done.30, f32[8,10,12,16,16]{3,4,2,1,0:T(8,128)} %copy.79, f32[8,10,12,16,16]{3,4,2,1,0:T(8,128)} %copy.78, pred[]{:T(512)S(6)} %eq.412), kind=kOutput, calls=%fused_computation.110 | convolution fusion | flops 60469760 | bytes 2044235 | tf_op jit(solution)/shard_map/gkc,gijcm->gijkm/dot_general | solution.py:157
  846.0 5.7 fusion.80
  861.1 9.8 %bitcast_add_fusion = f32[16,24,16,16]{1,3,0,2:T(8,128)} fusion(f32[24,16,16,16,1]{0,3,4,2,1:T(8,128)} %fusion.6, f32[24,16,16,16,1]{0,3,4,2,1:T(8,128)} %fusion.8, f32[24,16,16,16,1]{0,3,4,2,1:T(8,128)S(1)} %copy-done.32, f32[24,16,16,16,1]{0,3,4,2,1:T(8,128)} %fusion.12, f32[24,16,16,16,1]{0,3,4,2,1:T(8,128)} %fusion.14, ...), kind=kOutput, calls=%fused_computation.38 | convolution fusion | flops 151879680 | bytes 11272192 | tf_op jit(solution)/shard_map/xpqm,pqyz->xyzm/dot_general | solution.py:88
  (202 shorter events, 243.7 us)
Async XLA Ops:
  0.0 8.0 copy-start.25
  1.0 42.6 %collective-permute-start = (bf16[4,24,16,16]{1,3,2,0:T(8,128)(2,1)S(1)}, bf16[4,24,16,16]{1,3,2,0:T(8,128)(2,1)S(1)}, u32[]{:S(2)}, u32[]{:S(2)}) collective-permute-start(bf16[4,24,16,16]{1,3,2,0:T(8,128)(2,1)S(1)} %bitcast.631), channel_id=1, source_target_pairs={{0,16},{1,17},{2,18},{3,19},{4,20},{5,21},{6,22},{7,23},{8,24},{9,... | collective-permute-start | bytes 147464 | tf_op jit(solution)/shard_map/ppermute | solution.py:17
  3.6 40.0 %collective-permute-start.1 = (bf16[4,24,16,16]{1,3,2,0:T(8,128)(2,1)S(1)}, bf16[4,24,16,16]{1,3,2,0:T(8,128)(2,1)S(1)}, u32[]{:S(2)}, u32[]{:S(2)}) collective-permute-start(bf16[4,24,16,16]{1,3,2,0:T(8,128)(2,1)S(1)} %bitcast.632), channel_id=1, source_target_pairs={{16,0},{17,1},{18,2},{19,3},{20,4},{21,5},{22,6},{23,7},{24,8},{25... | collective-permute-start | bytes 147464 | tf_op jit(solution)/shard_map/ppermute | solution.py:19
  49.4 40.2 %collective-permute-start.2 = (bf16[24,4,16,16]{0,3,2,1:T(8,128)(2,1)S(1)}, bf16[24,4,16,16]{0,3,2,1:T(8,128)(2,1)}, u32[]{:S(2)}, u32[]{:S(2)}) collective-permute-start(bf16[24,4,16,16]{0,3,2,1:T(8,128)(2,1)S(1)} %copy.19), channel_id=1, source_target_pairs={{0,8},{1,9},{2,10},{3,11},{4,12},{5,13},{6,14},{7,15},{16,24},{17,... | collective-permute-start | bytes 147464 | tf_op jit(solution)/shard_map/ppermute | solution.py:17
  57.2 36.4 %collective-permute-start.3 = (bf16[24,4,16,16]{0,3,2,1:T(8,128)(2,1)}, bf16[24,4,16,16]{0,3,2,1:T(8,128)(2,1)}, u32[]{:S(2)}, u32[]{:S(2)}) collective-permute-start(bf16[24,4,16,16]{0,3,2,1:T(8,128)(2,1)} %copy.20), channel_id=1, source_target_pairs={{8,0},{9,1},{10,2},{11,3},{12,4},{13,5},{14,6},{15,7},{24,16},{25,... | collective-permute-start | bytes 147464 | tf_op jit(solution)/shard_map/ppermute | solution.py:19
  69.2 7.5 copy-start.8
  98.1 23.2 %copy-start = (bf16[24,4,16,16]{1,3,2,0:T(8,128)(2,1)S(1)}, bf16[24,4,16,16]{1,3,2,0:T(8,128)(2,1)}, u32[]{:S(2)}) copy-start(bf16[24,4,16,16]{1,3,2,0:T(8,128)(2,1)} %copy.22) | copy-start | bytes 147460
  100.1 21.2 %collective-permute-start.4 = (bf16[24,32,4,16]{1,3,2,0:T(8,128)(2,1)S(1)}, bf16[24,32,4,16]{1,3,2,0:T(8,128)(2,1)S(1)}, u32[]{:S(2)}, u32[]{:S(2)}) collective-permute-start(bf16[24,32,4,16]{1,3,2,0:T(8,128)(2,1)S(1)} %get-tuple-element.5), channel_id=1, source_target_pairs={{0,1},{1,2},{2,3},{3,4},{4,5},{5,6},{6,7},{8,9},{9,10},{10,11},{11... | collective-permute-start | bytes 294920 | tf_op jit(solution)/shard_map/ppermute | solution.py:17
  103.6 17.8 %collective-permute-start.5 = (bf16[24,32,4,16]{1,3,2,0:T(8,128)(2,1)S(1)}, bf16[24,32,4,16]{1,3,2,0:T(8,128)(2,1)S(1)}, u32[]{:S(2)}, u32[]{:S(2)}) collective-permute-start(bf16[24,32,4,16]{1,3,2,0:T(8,128)(2,1)S(1)} %get-tuple-element.6), channel_id=1, source_target_pairs={{1,0},{2,1},{3,2},{4,3},{5,4},{6,5},{7,6},{9,8},{10,9},{11,10},{12... | collective-permute-start | bytes 294920 | tf_op jit(solution)/shard_map/ppermute | solution.py:19
  123.9 9.6 %copy-start.4 = (bf16[24,32,24,16]{1,3,2,0:T(8,128)(2,1)}, bf16[24,32,24,16]{1,3,2,0:T(8,128)(2,1)S(1)}, u32[]{:S(2)}) copy-start(bf16[24,32,24,16]{1,3,2,0:T(8,128)(2,1)S(1)} %pad_maximum_fusion.1) | copy-start | bytes 1769476
  141.5 34.7 %collective-permute-start.6 = (bf16[6,12,8,16]{3,2,1,0:T(8,128)(2,1)S(1)}, bf16[6,12,8,16]{3,2,1,0:T(8,128)(2,1)S(1)}, u32[]{:S(2)}, u32[]{:S(2)}) collective-permute-start(bf16[6,12,8,16]{3,2,1,0:T(8,128)(2,1)S(1)} %get-tuple-element.13), channel_id=1, source_target_pairs={{0,16},{1,17},{2,18},{3,19},{4,20},{5,21},{6,22},{7,23},{8,24},{9,... | collective-permute-start | bytes 55304 | tf_op jit(solution)/shard_map/ppermute | solution.py:17
  143.4 8.2 copy-start.5
  143.4 8.2 copy-start.16
  143.4 32.8 %collective-permute-start.7 = (bf16[6,12,8,16]{3,2,1,0:T(8,128)(2,1)S(1)}, bf16[6,12,8,16]{3,2,1,0:T(8,128)(2,1)S(1)}, u32[]{:S(2)}, u32[]{:S(2)}) collective-permute-start(bf16[6,12,8,16]{3,2,1,0:T(8,128)(2,1)S(1)} %get-tuple-element.14), channel_id=1, source_target_pairs={{16,0},{17,1},{18,2},{19,3},{20,4},{21,5},{22,6},{23,7},{24,8},{25... | collective-permute-start | bytes 55304 | tf_op jit(solution)/shard_map/ppermute | solution.py:19
  171.0 11.4 %copy-start.11 = (bf16[32,24,24,16,1]{0,3,2,1,4:T(8,128)(2,1)S(1)}, bf16[32,24,24,16,1]{0,3,2,1,4:T(8,128)(2,1)}, u32[]{:S(2)}) copy-start(bf16[32,24,24,16,1]{0,3,2,1,4:T(8,128)(2,1)} %convert_bitcast_fusion.2) | copy-start | bytes 1769476
  176.4 10.9 %collective-permute-start.8 = (bf16[20,6,8,16]{3,2,1,0:T(8,128)(2,1)S(1)}, bf16[20,6,8,16]{3,2,1,0:T(8,128)(2,1)S(1)}, u32[]{:S(2)}, u32[]{:S(2)}) collective-permute-start(bf16[20,6,8,16]{3,2,1,0:T(8,128)(2,1)S(1)} %get-tuple-element.11), channel_id=1, source_target_pairs={{0,8},{1,9},{2,10},{3,11},{4,12},{5,13},{6,14},{7,15},{16,24},{17,... | collective-permute-start | bytes 92168 | tf_op jit(solution)/shard_map/ppermute | solution.py:17
  181.1 10.6 %collective-permute-start.9 = (bf16[20,6,8,16]{3,2,1,0:T(8,128)(2,1)S(1)}, bf16[20,6,8,16]{3,2,1,0:T(8,128)(2,1)S(1)}, u32[]{:S(2)}, u32[]{:S(2)}) collective-permute-start(bf16[20,6,8,16]{3,2,1,0:T(8,128)(2,1)S(1)} %get-tuple-element.12), channel_id=1, source_target_pairs={{8,0},{9,1},{10,2},{11,3},{12,4},{13,5},{14,6},{15,7},{24,16},{25,... | collective-permute-start | bytes 92168 | tf_op jit(solution)/shard_map/ppermute | solution.py:19
  195.3 25.6 %collective-permute-start.10 = (bf16[20,24,6,16]{1,3,2,0:T(8,128)(2,1)S(1)}, bf16[20,24,6,16]{1,3,2,0:T(8,128)(2,1)}, u32[]{:S(2)}, u32[]{:S(2)}) collective-permute-start(bf16[20,24,6,16]{1,3,2,0:T(8,128)(2,1)S(1)} %copy.43), channel_id=1, source_target_pairs={{0,1},{1,2},{2,3},{3,4},{4,5},{5,6},{6,7},{8,9},{9,10},{10,11},{11... | collective-permute-start | bytes 276488 | tf_op jit(solution)/shard_map/ppermute | solution.py:17
  202.8 20.5 %collective-permute-start.11 = (bf16[20,24,6,16]{1,3,2,0:T(8,128)(2,1)}, bf16[20,24,6,16]{1,3,2,0:T(8,128)(2,1)}, u32[]{:S(2)}, u32[]{:S(2)}) collective-permute-start(bf16[20,24,6,16]{1,3,2,0:T(8,128)(2,1)} %copy.44), channel_id=1, source_target_pairs={{1,0},{2,1},{3,2},{4,3},{5,4},{6,5},{7,6},{9,8},{10,9},{11,10},{12... | collective-permute-start | bytes 276488 | tf_op jit(solution)/shard_map/ppermute | solution.py:19
  280.9 45.2 %collective-permute-start.12 = (f32[8,10,12,4,16]{4,0,3,2,1:T(8,128)}, f32[8,10,12,4,16]{4,0,3,2,1:T(8,128)}, u32[]{:S(2)}, u32[]{:S(2)}) collective-permute-start(f32[8,10,12,4,16]{4,0,3,2,1:T(8,128)} %copy.71), channel_id=1, source_target_pairs={{0,1},{1,0},{2,3},{3,2},{4,5},{5,4},{6,7},{7,6},{8,9},{9,8},{10,11... | collective-permute-start | bytes 737288 | tf_op jit(solution)/shard_map/ppermute | solution.py:150
  335.7 9.0 %copy-start.3 = (bf16[20,24,20,16]{3,2,1,0:T(8,128)(2,1)S(1)}, bf16[20,24,20,16]{3,2,1,0:T(8,128)(2,1)}, u32[]{:S(2)}) copy-start(bf16[20,24,20,16]{3,2,1,0:T(8,128)(2,1)} %copy-done.1) | copy-start | bytes 921604
  343.0 85.9 %collective-permute-start.13 = (f32[8,10,12,8,16]{4,3,2,1,0:T(8,128)}, f32[8,10,12,8,16]{4,3,2,1,0:T(8,128)}, u32[]{:S(2)}, u32[]{:S(2)}) collective-permute-start(f32[8,10,12,8,16]{4,3,2,1,0:T(8,128)} %copy.74), channel_id=1, source_target_pairs={{0,2},{1,3},{2,0},{3,1},{4,6},{5,7},{6,4},{7,5},{8,10},{9,11},{10,... | collective-permute-start | bytes 1474568 | tf_op jit(solution)/shard_map/ppermute | solution.py:150
  463.0 338.7 %collective-permute-start.14 = (f32[8,10,12,16,16]{4,3,2,1,0:T(8,128)}, f32[8,10,12,16,16]{4,3,2,1,0:T(8,128)}, u32[]{:S(2)}, u32[]{:S(2)}) collective-permute-start(f32[8,10,12,16,16]{4,3,2,1,0:T(8,128)} %copy.77), channel_id=1, source_target_pairs={{0,4},{1,5},{2,6},{3,7},{4,0},{5,1},{6,2},{7,3},{8,12},{9,13},{10,... | collective-permute-start | bytes 2949128 | tf_op jit(solution)/shard_map/ppermute | solution.py:150
  483.6 327.1 %copy-start.30 = (pred[10]{0:T(512)(128)(4,1)S(1)}, pred[10]{0:T(512)(128)(4,1)}, u32[]{:S(2)}) copy-start(pred[10]{0:T(512)(128)(4,1)} %compare_and_fusion) | copy-start | bytes 34
  (24 other events, 108.4 us)
